TPU v7x, 256 devices: a whole 4x4x8 slice. The times are simulated.
256 devices in a mesh: wide: 64 (over z, x, y_lo), narrow: 4 (over y_hi, core).
Axes of the slice: x: 4, y: 4 (y_hi: 2, y_lo: 2; y = y_hi * 2 + y_lo), z: 8, core: 2. Of those that a mesh axis runs over, the one named last changes fastest.
Arguments:
- density: bfloat16 [8192, 8, 128], P(('wide', 'narrow')), may hold values from -6 to 6
- basis: bfloat16 [8192, 64, 128], P(('wide', 'narrow')), may hold values from -0.5 to 0.5
- near_list: int32 [8192, 6], P(('wide', 'narrow')), may hold values from 0 to 8191, as said below
- near_blocks: bfloat16 [8192, 6, 128, 128], P(('wide', 'narrow')), may hold values from -0.21875 to 0.21875
- far_leaf: int32 [8192, 6], P(('wide', 'narrow')), may hold values from 0 to 8191, as said below
- leaf_coupling: bfloat16 [8192, 64, 384], P(('wide', 'narrow')), may hold values from -0.3125 to 0.3125
- transfer: bfloat16 [1024, 64, 512], P(('wide', 'narrow')), may hold values from -0.75 to 0.75
- far_coarse: int32 [1024, 8], P(('wide', 'narrow')), may hold values from 0 to 1023
- coarse_coupling: bfloat16 [1024, 64, 512], P(('wide', 'narrow')), may hold values from -0.25 to 0.25
Outputs:
- potential: bfloat16 [8192, 8, 128], P(('wide', 'narrow'))
Inputs may be any that keep to these rules, and one draw needn't show every extreme that they name: `near_list`: every entry lies within 32 leaves of its own leaf l; the first entry is l itself. `far_leaf`: every entry lies within 32 leaves of its own leaf.
All inputs are finite; a program needn't handle non-finite values.
Results may differ from a plain program's by a relative error of at most 0.0066.
Values may be sent and summed in bfloat16 or wider, within the bound.
No kernel may reach another device: no remote copies, remote signals or barrier semaphores. Data moves between devices by JAX's collectives and lax.ppermute only.
A program may use at most 64 MiB of HBM per device.

v0:
```python
import jax
import jax.numpy as jnp
from jax import lax
from jax.sharding import PartitionSpec as P


def with_halo(block, sides, width):
    for axis, dim in sides:
        count = lax.axis_size(axis)
        forward = [(i, i + 1) for i in range(count - 1)]
        backward = [(target, source) for source, target in forward]
        low = lax.ppermute(
            lax.slice_in_dim(block, block.shape[dim] - width, None, axis=dim), axis, forward
        )
        high = lax.ppermute(lax.slice_in_dim(block, 0, width, axis=dim), axis, backward)
        block = jnp.concatenate([low, block, high], axis=dim)
    return block


def body(
    density,
    basis,
    near_list,
    near_blocks,
    far_leaf,
    leaf_coupling,
    transfer,
    far_coarse,
    coarse_coupling,
):
    leaf_count, rhs_count, leaf_width = density.shape
    rank_width = basis.shape[1]
    box_count = transfer.shape[0]
    child_count = leaf_count // box_count
    far_count = far_leaf.shape[1]
    coarse_count = far_coarse.shape[1]
    skeleton = jnp.einsum(
        "lrp,lkp->lrk", density, basis, preferred_element_type=jnp.float32
    ).astype(jnp.bfloat16)
    children = skeleton.reshape(box_count, child_count, rhs_count, rank_width)
    coarse = jnp.einsum(
        "ckim,cirm->crk",
        transfer.reshape(box_count, rank_width, child_count, rank_width),
        children,
        preferred_element_type=jnp.float32,
    ).astype(jnp.bfloat16)
    coarse_flat = coarse.reshape(box_count, rhs_count * rank_width)
    everything = lax.all_gather(coarse_flat, ("wide", "narrow"), axis=0, tiled=True)
    offset_base = lax.axis_index(("wide", "narrow")) * leaf_count - leaf_count
    density_flat = density.reshape(leaf_count, rhs_count * leaf_width)
    skeleton_flat = skeleton.reshape(leaf_count, rhs_count * rank_width)
    density_padded = with_halo(density_flat, ((("wide", "narrow"), 0),), leaf_count)
    skeleton_padded = with_halo(skeleton_flat, ((("wide", "narrow"), 0),), leaf_count)
    near_rows = jnp.take(density_padded, near_list - offset_base, axis=0).reshape(
        leaf_count, near_list.shape[1], rhs_count, leaf_width
    )
    near_part = jnp.einsum(
        "ljpq,ljrq->lrp", near_blocks, near_rows, preferred_element_type=jnp.float32
    )
    far_skels = jnp.take(skeleton_padded, far_leaf - offset_base, axis=0).reshape(
        leaf_count, far_count, rhs_count, rank_width
    )
    leaf_far = jnp.einsum(
        "lkjm,ljrm->lrk",
        leaf_coupling.reshape(leaf_count, rank_width, far_count, rank_width),
        far_skels,
        preferred_element_type=jnp.float32,
    )
    coarse_skels = jnp.take(everything, far_coarse, axis=0).reshape(
        box_count, coarse_count, rhs_count, rank_width
    )
    coarse_field = jnp.einsum(
        "ckjm,cjrm->crk",
        coarse_coupling.reshape(box_count, rank_width, coarse_count, rank_width),
        coarse_skels,
        preferred_element_type=jnp.float32,
    ).astype(jnp.bfloat16)
    descended = jnp.einsum(
        "ckim,crk->cirm",
        transfer.reshape(box_count, rank_width, child_count, rank_width),
        coarse_field,
        preferred_element_type=jnp.float32,
    ).reshape(leaf_count, rhs_count, rank_width)
    local_field = (leaf_far + descended).astype(jnp.bfloat16)
    total = (
        jnp.einsum("lrk,lkp->lrp", local_field, basis, preferred_element_type=jnp.float32)
        + near_part
    )
    return total.astype(jnp.bfloat16)


def solution(mesh):
    return jax.shard_map(
        body,
        mesh=mesh,
        in_specs=(
            P(("wide", "narrow"), None, None),
            P(("wide", "narrow"), None, None),
            P(("wide", "narrow"), None),
            P(("wide", "narrow"), None, None, None),
            P(("wide", "narrow"), None),
            P(("wide", "narrow"), None, None),
            P(("wide", "narrow"), None, None),
            P(("wide", "narrow"), None),
            P(("wide", "narrow"), None, None),
        ),
        out_specs=P(("wide", "narrow"), None, None),
        check_vma=False,
    )
```

profile of v0, /device:TPU:1, one launch (start us, length us, event | category | flops | bytes accessed | tf_op | source)
XLA Modules:
  0.0 415.8 jit_solution(6221959910823239641)
XLA Ops:
  6.5 1.4 reshape.49
  8.0 1.2 convolution_convert_fusion
  9.2 0.3 fusion.16
  9.4 0.7 reshape.87
  10.2 0.1 reshape.46
  10.3 6.2 %collective-permute-start = (bf16[32,512]{1,0:T(8,128)(2,1)S(1)}, bf16[32,512]{1,0:T(8,128)(2,1)S(1)}, u32[]{:S(2)}, u32[]{:S(2)}) collective-permute-start(bf16[32,512]{1,0:T(8,128)(2,1)S(1)} %reshape.46), channel_id=1, source_target_pairs={{0,1},{1,2},{2,3},{3,4},{4,5},{5,6},{6,7},{7,8},{8,9},{9,10},{10,1... | collective-permute-start | bytes 98312 | tf_op jit(solution)/shard_map/ppermute | solution.py:12
  16.5 1.9 collective-permute-start.1
  18.4 0.9 copy.53
  19.3 5.1 %collective-permute-start.2 = (bf16[32,1024]{1,0:T(8,128)(2,1)S(1)}, bf16[32,1024]{1,0:T(8,128)(2,1)S(1)}, u32[]{:S(2)}, u32[]{:S(2)}) collective-permute-start(bf16[32,1024]{1,0:T(8,128)(2,1)S(1)} %bitcast.57), channel_id=1, source_target_pairs={{0,1},{1,2},{2,3},{3,4},{4,5},{5,6},{6,7},{7,8},{8,9},{9,10},{10,1... | collective-permute-start | bytes 196616 | tf_op jit(solution)/shard_map/ppermute | solution.py:12
  24.4 1.9 collective-permute-start.3
  26.4 0.7 compare_and_fusion
  27.1 0.1 copy.21
  27.2 0.1 reshape.56
  27.3 0.7 compare_select_fusion.2
  27.9 0.1 reshape.64
  28.0 0.1 copy.27
  28.1 0.1 reshape.72
  28.3 0.7 compare_and_fusion.2
  29.0 0.1 copy.20
  29.1 1.3 reshape.51
  30.3 3.7 reshape.47
  34.1 0.1 copy.26
  34.2 1.0 gather_fusion
  35.2 0.2 gather.19
  35.5 1.0 gather_fusion.2
  36.6 361.3 %all-gather.3.cloned.1.call-done = bf16[256,4,512]{2,1,0:T(4,128)(2,1)} async-done(((bf16[1,4,512]{2,1,0:T(4,128)(2,1)}), bf16[256,4,512]{2,1,0:T(4,128)(2,1)}) %all-gather.3.cloned.1.call-update) | async-done | bytes 1048592 | tf_op jit(solution)/shard_map/all_gather | solution.py:48
  397.9 1.3 reshape.88
  399.2 0.6 gather_fusion.1
  399.8 0.1 gather.21
  399.9 0.4 fusion.19
  400.4 3.4 fusion.14
  403.8 5.2 %fusion.12 = bf16[32,8,128]{2,1,0:T(8,128)(2,1)} fusion(f32[32,8,128]{2,1,0:T(8,128)S(1)} %fusion.14, bf16[32,6,128,128]{3,2,1,0:T(8,128)(2,1)} %param.12, bf16[32,6,8,128]{3,2,1,0:T(8,128)(2,1)S(1)} %bitcast.53, pred[32,6]{1,0:T(8,128)(4,1)S(1)} %copy.26), kind=kOutput, calls=%fused_computation.10 | convolution fusion | flops 50593792 | bytes 6881472 | tf_op jit(solution)/shard_map/ljpq,ljrq->lrp/dot_general | solution.py:57
  (16 shorter events, 0.1 us)
Async XLA Ops:
  6.5 1.4 copy-start
  6.5 23.8 %copy-start.1 = (bf16[32,64,384]{2,1,0:T(8,128)(2,1)S(1)}, bf16[32,64,384]{2,1,0:T(8,128)(2,1)}, u32[]{:S(2)}) copy-start(bf16[32,64,384]{2,1,0:T(8,128)(2,1)} %param.14) | copy-start | bytes 4718596
  6.5 391.3 %all-gather.3.cloned.1.call-start = ((), (), s32[]{:S(2)}) async-start(), calls=%async_computation | async-start | bytes 1052672 | tf_op jit(solution)/shard_map/all_gather | solution.py:48
  10.3 23.9 %collective-permute-start = (bf16[32,512]{1,0:T(8,128)(2,1)S(1)}, bf16[32,512]{1,0:T(8,128)(2,1)S(1)}, u32[]{:S(2)}, u32[]{:S(2)}) collective-permute-start(bf16[32,512]{1,0:T(8,128)(2,1)S(1)} %reshape.46), channel_id=1, source_target_pairs={{0,1},{1,2},{2,3},{3,4},{4,5},{5,6},{6,7},{7,8},{8,9},{9,10},{10,1... | collective-permute-start | bytes 98312 | tf_op jit(solution)/shard_map/ppermute | solution.py:12
  16.5 17.7 %collective-permute-start.1 = (bf16[32,512]{1,0:T(8,128)(2,1)S(1)}, bf16[32,512]{1,0:T(8,128)(2,1)S(1)}, u32[]{:S(2)}, u32[]{:S(2)}) collective-permute-start(bf16[32,512]{1,0:T(8,128)(2,1)S(1)} %reshape.46), channel_id=1, source_target_pairs={{1,0},{2,1},{3,2},{4,3},{5,4},{6,5},{7,6},{8,7},{9,8},{10,9},{11,1... | collective-permute-start | bytes 98312 | tf_op jit(solution)/shard_map/ppermute | solution.py:15
  19.3 16.2 %collective-permute-start.2 = (bf16[32,1024]{1,0:T(8,128)(2,1)S(1)}, bf16[32,1024]{1,0:T(8,128)(2,1)S(1)}, u32[]{:S(2)}, u32[]{:S(2)}) collective-permute-start(bf16[32,1024]{1,0:T(8,128)(2,1)S(1)} %bitcast.57), channel_id=1, source_target_pairs={{0,1},{1,2},{2,3},{3,4},{4,5},{5,6},{6,7},{7,8},{8,9},{9,10},{10,1... | collective-permute-start | bytes 196616 | tf_op jit(solution)/shard_map/ppermute | solution.py:12
  24.4 11.0 %collective-permute-start.3 = (bf16[32,1024]{1,0:T(8,128)(2,1)S(1)}, bf16[32,1024]{1,0:T(8,128)(2,1)S(1)}, u32[]{:S(2)}, u32[]{:S(2)}) collective-permute-start(bf16[32,1024]{1,0:T(8,128)(2,1)S(1)} %bitcast.58), channel_id=1, source_target_pairs={{1,0},{2,1},{3,2},{4,3},{5,4},{6,5},{7,6},{8,7},{9,8},{10,9},{11,1... | collective-permute-start | bytes 196616 | tf_op jit(solution)/shard_map/ppermute | solution.py:15
Sparse Core Ops, SparseCore 0:
  10.3 387.5 all-gather.2
where the time goes:
time: 416 us
  waiting for transfers between devices  361 us (87%)
  starting transfers between devices  15.2 us (4%)
  between operations  13.6 us (3%)
  local copies, waits for them, and re-layouts  13.1 us (3%)
  matrix products  10.5 us (3%)
    all_gather x1, waiting for transfers between devices, body(): lax.all_gather(coarse_flat, ('wide', 'narrow'), axis=0, tiled=True)  361 us
    ppermute x2, starting transfers between devices, with_halo(): lax.ppermute(lax.slice_in_dim(block, block.shape[dim] - width, None, axis...  11.3 us
  transfers between devices with their start and end apart: 5, of which 1 were waited for; matrix products, arithmetic and copies ran while one was open for 3% of the time, Pallas kernels for 0%

commit v1 on v0

--- a/solution.py
+++ b/solution.py
@@ -45,7 +45,12 @@
         preferred_element_type=jnp.float32,
     ).astype(jnp.bfloat16)
     coarse_flat = coarse.reshape(box_count, rhs_count * rank_width)
-    everything = lax.all_gather(coarse_flat, ("wide", "narrow"), axis=0, tiled=True)
+    everything = jnp.concatenate(
+        lax.all_to_all(
+            jnp.stack([coarse_flat] * lax.axis_size(("wide", "narrow"))), ("wide", "narrow"), 0, 0
+        ),
+        axis=0,
+    )
     offset_base = lax.axis_index(("wide", "narrow")) * leaf_count - leaf_count
     density_flat = density.reshape(leaf_count, rhs_count * leaf_width)
     skeleton_flat = skeleton.reshape(leaf_count, rhs_count * rank_width)

time: 416 us -> 63.4 us (0.15)
  waiting for transfers between devices: 361 us -> 7.64 us
  starting transfers between devices: 15.2 us -> 29.7 us
  between operations: 13.6 us -> 0.23 us
    all_gather x1 -> x0, waiting for transfers between devices: 361 us -> none  [body(): lax.all_gather(coarse_flat, ('wide', 'narrow'), axis=0, tiled=True)]
    all_to_all x0 -> x1, starting transfers between devices: none -> 15.6 us  [body(): lax.all_to_all(jnp.stack([coarse_flat] * lax.axis_size(('wide', 'narrow')...]
    all_to_all x0 -> x1, waiting for transfers between devices: none -> 7.63 us  [body(): lax.all_to_all(jnp.stack([coarse_flat] * lax.axis_size(('wide', 'narrow')...]
  transfers between devices with their start and end apart: 5 -> 5, of which waited for: 1 -> 1; matrix products, arithmetic and copies ran while one was open for 3% -> 15% of each run, Pallas kernels for 0% -> 0%
where the time goes in v1:
time: 63.4 us; the launch traced here: 63 us
  starting transfers between devices  29.7 us (47%)
  local copies, waits for them, and re-layouts  15.1 us (24%)
  matrix products  10.2 us (16%)
  waiting for transfers between devices  7.64 us (12%)
    all_to_all x1, starting transfers between devices, body(): lax.all_to_all(jnp.stack([coarse_flat] * lax.axis_size(('wide', 'narrow')...  15.6 us
    ppermute x2, starting transfers between devices, with_halo(): lax.ppermute(lax.slice_in_dim(block, block.shape[dim] - width, None, axis...  10.2 us
    all_to_all x1, waiting for transfers between devices, body(): lax.all_to_all(jnp.stack([coarse_flat] * lax.axis_size(('wide', 'narrow')...  7.63 us
    dot_general x1, matrix products, body(): jnp.einsum('ljpq,ljrq->lrp', near_blocks, near_rows, preferred_element_ty...  5.2 us
    reshape x1, local copies, waits for them, and re-layouts, body(): leaf_coupling.reshape(leaf_count, rank_width, far_count, rank_width)  4.18 us
    ppermute x2, starting transfers between devices, with_halo(): lax.ppermute(lax.slice_in_dim(block, 0, width, axis=dim), axis, backward)  3.84 us
    dot_general x1, matrix products, body(): jnp.einsum('lrk,lkp->lrp', local_field, basis, preferred_element_type=jnp...  3.09 us
    gather x2, local copies, waits for them, and re-layouts, body(): jnp.take(everything, far_coarse, axis=0)  2.14 us
  transfers between devices with their start and end apart: 5, of which 1 were waited for; matrix products, arithmetic and copies ran while one was open for 15% of the time, Pallas kernels for 0%

profile of v1, /device:TPU:1, one launch (start us, length us, event | category | flops | bytes accessed | tf_op | source)
XLA Modules:
  0.0 63.0 jit_solution(6943628366080971511)
XLA Ops:
  0.0 1.3 %reshape.51 = bf16[4,64,8,64]{3,2,1,0:T(8,128)(2,1)S(1)} reshape(bf16[4,64,512]{2,1,0:T(8,128)(2,1)} %param.15) | data formatting | bytes 524288 | tf_op jit(solution)/shard_map/reshape | solution.py:43
  1.4 1.2 %convolution_convert_fusion = bf16[32,8,64]{2,1,0:T(8,128)(2,1)S(1)} fusion(bf16[32,8,128]{2,1,0:T(8,128)(2,1)} %param.9, bf16[32,64,128]{2,1,0:T(8,128)(2,1)S(1)} %copy-done), kind=kOutput, calls=%fused_computation.9 | convolution fusion | flops 4210688 | bytes 622592 | tf_op jit(solution)/shard_map/lrp,lkp->lrk/dot_general | solution.py:37
  2.6 0.3 fusion.5
  2.9 0.1 stack_reshape.2
  2.9 1.3 %stack.3 = bf16[256,4,512]{2,1,0:T(4,128)(2,1)} broadcast(bf16[4,512]{1,0:T(4,128)(2,1)S(1)} %stack_reshape.2), dimensions={1,2} | broadcast | bytes 1052672 | tf_op jit(solution)/shard_map/stack | solution.py:50
  4.2 15.6 %all-to-all-start = ((bf16[256,4,512]{2,1,0:T(4,128)(2,1)}), bf16[256,4,512]{2,1,0:T(4,128)(2,1)S(1)}, u32[]{:S(2)}, u32[]{:S(2)}) async-start(bf16[256,4,512]{2,1,0:T(4,128)(2,1)} %stack.3), calls=%async_computation | async-start | bytes 2097152 | tf_op jit(solution)/shard_map/all_to_all | solution.py:49
  19.9 0.1 reshape.48
  20.0 5.0 %collective-permute-start = (bf16[32,512]{1,0:T(8,128)(2,1)S(1)}, bf16[32,512]{1,0:T(8,128)(2,1)S(1)}, u32[]{:S(2)}, u32[]{:S(2)}) collective-permute-start(bf16[32,512]{1,0:T(8,128)(2,1)S(1)} %reshape.48), channel_id=1, source_target_pairs={{0,1},{1,2},{2,3},{3,4},{4,5},{5,6},{6,7},{7,8},{8,9},{9,10},{10,1... | collective-permute-start | bytes 98312 | tf_op jit(solution)/shard_map/ppermute | solution.py:12
  25.1 1.9 %collective-permute-start.1 = (bf16[32,512]{1,0:T(8,128)(2,1)S(1)}, bf16[32,512]{1,0:T(8,128)(2,1)S(1)}, u32[]{:S(2)}, u32[]{:S(2)}) collective-permute-start(bf16[32,512]{1,0:T(8,128)(2,1)S(1)} %reshape.48), channel_id=1, source_target_pairs={{1,0},{2,1},{3,2},{4,3},{5,4},{6,5},{7,6},{8,7},{9,8},{10,9},{11,1... | collective-permute-start | bytes 98312 | tf_op jit(solution)/shard_map/ppermute | solution.py:15
  27.0 5.1 %collective-permute-start.2 = (bf16[32,1024]{1,0:T(8,128)(2,1)S(1)}, bf16[32,1024]{1,0:T(8,128)(2,1)S(1)}, u32[]{:S(2)}, u32[]{:S(2)}) collective-permute-start(bf16[32,1024]{1,0:T(8,128)(2,1)S(1)} %bitcast.63), channel_id=1, source_target_pairs={{0,1},{1,2},{2,3},{3,4},{4,5},{5,6},{6,7},{7,8},{8,9},{9,10},{10,1... | collective-permute-start | bytes 196616 | tf_op jit(solution)/shard_map/ppermute | solution.py:12
  32.2 1.9 %collective-permute-start.3 = (bf16[32,1024]{1,0:T(8,128)(2,1)S(1)}, bf16[32,1024]{1,0:T(8,128)(2,1)S(1)}, u32[]{:S(2)}, u32[]{:S(2)}) collective-permute-start(bf16[32,1024]{1,0:T(8,128)(2,1)S(1)} %bitcast.64), channel_id=1, source_target_pairs={{1,0},{2,1},{3,2},{4,3},{5,4},{6,5},{7,6},{8,7},{9,8},{10,9},{11,1... | collective-permute-start | bytes 196616 | tf_op jit(solution)/shard_map/ppermute | solution.py:15
  34.1 0.1 copy.15
  34.2 0.1 reshape.58
  34.4 0.1 reshape.66
  34.4 0.1 copy.19
  34.5 0.1 reshape.74
  34.7 0.1 copy.14
  34.8 0.3 copy.28
  35.1 4.2 %copy.27 = bf16[32,64,384]{1,2,0:T(8,128)(2,1)} copy(bf16[32,64,384]{2,1,0:T(8,128)(2,1)} %param.14) | data formatting | bytes 3145728 | tf_op jit(solution)/shard_map/reshape | solution.py:70
  39.3 0.1 copy.18
  39.4 0.0 collective-permute-done.1
  39.4 1.0 %gather_fusion = bf16[192,512]{1,0:T(8,128)(2,1)S(1)} fusion(bf16[96,512]{1,0:T(8,128)(2,1)S(1)} %pad_maximum_fusion.1, s32[1024]{0:T(1024)S(1)} %pad_clamp_fusion.2), kind=kCustom, calls=%fused_computation | custom fusion | bytes 393984 | tf_op jit(solution)/shard_map/jit(_take)/gather | solution.py:65
  40.4 1.0 %gather.19 = bf16[32,6,8,64]{3,2,1,0:T(8,128)(2,1)} reshape(bf16[192,512]{1,0:T(8,128)(2,1)S(1)} %gather_fusion) | data formatting | bytes 393216 | tf_op jit(solution)/shard_map/jit(_take)/gather | solution.py:65
  41.4 1.0 %gather_fusion.2 = bf16[192,1024]{1,0:T(8,128)(2,1)S(1)} fusion(bf16[96,1024]{1,0:T(8,128)(2,1)S(1)} %pad_maximum_fusion, s32[1024]{0:T(1024)S(1)} %pad_clamp_fusion), kind=kCustom, calls=%fused_computation.2 | custom fusion | bytes 787200 | tf_op jit(solution)/shard_map/jit(_take)/gather | solution.py:59
  42.5 0.8 %copy.30 = bf16[24,8,8,128]{3,2,1,0:T(8,128)(2,1)} copy(bf16[24,8,8,128]{3,1,2,0:T(8,128)(2,1)S(1)} %bitcast.57) | data formatting | bytes 786432
  43.3 7.6 %all-to-all-done = bf16[256,4,512]{2,1,0:T(4,128)(2,1)S(1)} async-done(((bf16[256,4,512]{2,1,0:T(4,128)(2,1)}), bf16[256,4,512]{2,1,0:T(4,128)(2,1)S(1)}, u32[]{:S(2)}, u32[]{:S(2)}) %all-to-all-start) | async-done | bytes 1048608 | tf_op jit(solution)/shard_map/all_to_all | solution.py:49
  50.9 1.1 %reshape.52 = bf16[1024,512]{1,0:T(8,128)(2,1)} reshape(bf16[256,4,512]{2,1,0:T(4,128)(2,1)S(1)} %all-to-all-done) | data formatting | bytes 2097152 | tf_op jit(solution)/shard_map/reshape | solution.py:48
  52.1 2.0 %gather_fusion.1 = bf16[32,512]{1,0:T(8,128)(2,1)S(1)} fusion(bf16[1024,512]{1,0:T(8,128)(2,1)} %reshape.52, s32[1024]{0:T(1024)S(1)} %pad_clamp_fusion.1), kind=kCustom, calls=%fused_computation.1 | custom fusion | bytes 65664 | tf_op jit(solution)/shard_map/jit(_take)/gather | solution.py:74
  54.1 0.1 gather.21
  54.2 0.5 fusion.8
  54.7 3.1 %fusion.4 = f32[32,8,128]{2,1,0:T(8,128)S(1)} fusion(bf16[32,64,128]{2,1,0:T(8,128)(2,1)S(1)} %copy-done, f32[32,8,64]{2,1,0:T(8,128)S(1)} %bitcast.61, bf16[32,64,6,64]{1,3,2,0:T(8,128)(2,1)} %bitcast.56, bf16[32,6,8,64]{3,2,1,0:T(8,128)(2,1)S(1)} %copy-done.1, pred[32,6]{1,0:T(8,128)(4,1)S(1)} %copy.14), kind=kOutput, calls=%fused_computation.10 | convolution fusion | flops 16908288 | bytes 2490560 | tf_op jit(solution)/shard_map/lrk,lkp->lrp/dot_general | solution.py:91
  57.8 5.2 %fusion.3 = bf16[32,8,128]{2,1,0:T(8,128)(2,1)} fusion(f32[32,8,128]{2,1,0:T(8,128)S(1)} %fusion.4, bf16[32,6,128,128]{3,2,1,0:T(8,128)(2,1)} %param.12, bf16[32,6,8,128]{3,2,1,0:T(8,128)(2,1)S(1)} %bitcast.59, pred[32,6]{1,0:T(8,128)(4,1)S(1)} %copy.18), kind=kOutput, calls=%fused_computation.8 | convolution fusion | flops 50593792 | bytes 6881472 | tf_op jit(solution)/shard_map/ljpq,ljrq->lrp/dot_general | solution.py:62
  (28 shorter events, 0.1 us)
Async XLA Ops:
  0.0 1.4 %copy-start = (bf16[32,64,128]{2,1,0:T(8,128)(2,1)S(1)}, bf16[32,64,128]{2,1,0:T(8,128)(2,1)}, u32[]{:S(2)}) copy-start(bf16[32,64,128]{2,1,0:T(8,128)(2,1)} %param.10) | copy-start | bytes 1572868
  0.0 27.0 %copy-start.4 = (bf16[32,8,128]{2,1,0:T(8,128)(2,1)S(1)}, bf16[32,8,128]{2,1,0:T(8,128)(2,1)}, u32[]{:S(2)}) copy-start(bf16[32,8,128]{2,1,0:T(8,128)(2,1)} %param.9) | copy-start | bytes 196612
  0.0 34.1 %copy-start.6 = (s32[32,6]{0,1:T(8,128)S(1)}, s32[32,6]{0,1:T(8,128)}, u32[]{:S(2)}) copy-start(s32[32,6]{0,1:T(8,128)} %param.11) | copy-start | bytes 2308
  0.0 34.1 %copy-start.7 = (s32[32,6]{0,1:T(8,128)S(1)}, s32[32,6]{0,1:T(8,128)}, u32[]{:S(2)}) copy-start(s32[32,6]{0,1:T(8,128)} %param.13) | copy-start | bytes 2308
  0.0 34.3 %copy-start.5 = (s32[4,8]{1,0:T(4,128)S(1)}, s32[4,8]{1,0:T(4,128)}, u32[]{:S(2)}) copy-start(s32[4,8]{1,0:T(4,128)} %param.16) | copy-start | bytes 388
  0.0 34.8 %copy-start.3 = (bf16[4,64,512]{2,1,0:T(8,128)(2,1)S(1)}, bf16[4,64,512]{2,1,0:T(8,128)(2,1)}, u32[]{:S(2)}) copy-start(bf16[4,64,512]{2,1,0:T(8,128)(2,1)} %param.17) | copy-start | bytes 786436
  4.2 46.7 %all-to-all-start = ((bf16[256,4,512]{2,1,0:T(4,128)(2,1)}), bf16[256,4,512]{2,1,0:T(4,128)(2,1)S(1)}, u32[]{:S(2)}, u32[]{:S(2)}) async-start(bf16[256,4,512]{2,1,0:T(4,128)(2,1)} %stack.3), calls=%async_computation | async-start | bytes 2097152 | tf_op jit(solution)/shard_map/all_to_all | solution.py:49
  20.0 19.4 %collective-permute-start = (bf16[32,512]{1,0:T(8,128)(2,1)S(1)}, bf16[32,512]{1,0:T(8,128)(2,1)S(1)}, u32[]{:S(2)}, u32[]{:S(2)}) collective-permute-start(bf16[32,512]{1,0:T(8,128)(2,1)S(1)} %reshape.48), channel_id=1, source_target_pairs={{0,1},{1,2},{2,3},{3,4},{4,5},{5,6},{6,7},{7,8},{8,9},{9,10},{10,1... | collective-permute-start | bytes 98312 | tf_op jit(solution)/shard_map/ppermute | solution.py:12
  25.1 14.3 %collective-permute-start.1 = (bf16[32,512]{1,0:T(8,128)(2,1)S(1)}, bf16[32,512]{1,0:T(8,128)(2,1)S(1)}, u32[]{:S(2)}, u32[]{:S(2)}) collective-permute-start(bf16[32,512]{1,0:T(8,128)(2,1)S(1)} %reshape.48), channel_id=1, source_target_pairs={{1,0},{2,1},{3,2},{4,3},{5,4},{6,5},{7,6},{8,7},{9,8},{10,9},{11,1... | collective-permute-start | bytes 98312 | tf_op jit(solution)/shard_map/ppermute | solution.py:15
  27.0 14.4 %collective-permute-start.2 = (bf16[32,1024]{1,0:T(8,128)(2,1)S(1)}, bf16[32,1024]{1,0:T(8,128)(2,1)S(1)}, u32[]{:S(2)}, u32[]{:S(2)}) collective-permute-start(bf16[32,1024]{1,0:T(8,128)(2,1)S(1)} %bitcast.63), channel_id=1, source_target_pairs={{0,1},{1,2},{2,3},{3,4},{4,5},{5,6},{6,7},{7,8},{8,9},{9,10},{10,1... | collective-permute-start | bytes 196616 | tf_op jit(solution)/shard_map/ppermute | solution.py:12
  32.2 9.3 %collective-permute-start.3 = (bf16[32,1024]{1,0:T(8,128)(2,1)S(1)}, bf16[32,1024]{1,0:T(8,128)(2,1)S(1)}, u32[]{:S(2)}, u32[]{:S(2)}) collective-permute-start(bf16[32,1024]{1,0:T(8,128)(2,1)S(1)} %bitcast.64), channel_id=1, source_target_pairs={{1,0},{2,1},{3,2},{4,3},{5,4},{6,5},{7,6},{8,7},{9,8},{10,9},{11,1... | collective-permute-start | bytes 196616 | tf_op jit(solution)/shard_map/ppermute | solution.py:15
  42.5 12.2 %copy-start.1 = (bf16[32,6,8,64]{3,2,1,0:T(8,128)(2,1)S(1)}, bf16[32,6,8,64]{3,2,1,0:T(8,128)(2,1)}, u32[]{:S(2)}) copy-start(bf16[32,6,8,64]{3,2,1,0:T(8,128)(2,1)} %gather.19) | copy-start | bytes 589828
  52.1 5.7 %copy-start.2 = (bf16[24,8,8,128]{3,2,1,0:T(8,128)(2,1)S(1)}, bf16[24,8,8,128]{3,2,1,0:T(8,128)(2,1)}, u32[]{:S(2)}) copy-start(bf16[24,8,8,128]{3,2,1,0:T(8,128)(2,1)} %copy.30) | copy-start | bytes 1179652
